TPU v7x, 256 devices: a whole 4x4x8 slice. The times are simulated.
256 devices in a mesh: dp: 8 (over x, core), expert: 16 (over y, z_hi), tensor: 2 (over z_lo).
Axes of the slice: x: 4, y: 4, z: 8 (z_hi: 4, z_lo: 2; z = z_hi * 2 + z_lo), core: 2. Of those that a mesh axis runs over, the one named last changes fastest.
Arguments:
- tokens: bfloat16 [1024, 7168], P(('dp', 'expert'), 'tensor'), may hold values from -6 to 6
- upstream: bfloat16 [1024, 7168], P(('dp', 'expert'), 'tensor'), may hold values from -3 to 3
- probs: bfloat16 [1024, 8], P(('dp', 'expert')), may hold values from 0.049804688 to 0.59765625
- routing: int32 [1024, 8], P(('dp', 'expert')), may hold values from 0 to 15, all different within a row; in each aligned block of 8 rows (0 to 7, 8 to 15, ...) at most 5 rows name the same one
- row_rollout: int32 [1024], P(('dp', 'expert')), may hold values from 0 to 255
- group_ids: int32 [256], replicated, may hold values from 0 to 31
- rewards: int32 [256], replicated, may hold values from 0 to 1
- w_gate: bfloat16 [16, 7168, 2048], P('expert', None, ('dp', 'tensor')), may hold values from -0.0625 to 0.0625
- w_up: bfloat16 [16, 7168, 2048], P('expert', None, ('dp', 'tensor')), may hold values from -0.0625 to 0.0625
- w_down: bfloat16 [16, 2048, 7168], P('expert', ('dp', 'tensor')), may hold values from -0.125 to 0.125
Outputs:
- input_grad: bfloat16 [1024, 7168], P(('dp', 'expert'), 'tensor')
- route_grad: bfloat16 [1024, 8], P(('dp', 'expert'))
- grad_gate: bfloat16 [16, 7168, 2048], P('expert', None, ('dp', 'tensor'))
- grad_up: bfloat16 [16, 7168, 2048], P('expert', None, ('dp', 'tensor'))
- grad_down: bfloat16 [16, 2048, 7168], P('expert', ('dp', 'tensor'))
Inputs may be any that keep to these rules, and one draw needn't show every extreme that they name: `routing`: each row names 8 different experts. Within each aligned block of 8 rows (the tokens of one index pair of dp and expert) no expert is named by more than 5 rows, a bound that some block reaches.
All inputs are finite; a program needn't handle non-finite values.
Results may differ from a plain program's by a relative error of at most 0.025.
Values may be sent and summed in bfloat16 or wider, within the bound.
No kernel may reach another device: no remote copies, remote signals or barrier semaphores. Data moves between devices by JAX's collectives and lax.ppermute only.
A program may use at most 128 MiB of HBM per device.

v0:
```python
import jax
import jax.numpy as jnp
from jax import lax
from jax.sharding import PartitionSpec as P


def advantages(row_rollout, group_ids, rewards):
    same_group = (group_ids[:, None] == group_ids[None, :]).astype(jnp.float32)
    reward_values = rewards.astype(jnp.float32)
    group_total = jnp.dot(same_group, reward_values, precision=lax.Precision.HIGHEST)
    group_count = jnp.sum(same_group, axis=1)
    per_rollout = reward_values - group_total / group_count
    member = (
        row_rollout[:, None] == jnp.arange(per_rollout.shape[0], dtype=jnp.int32)[None, :]
    ).astype(jnp.float32)
    return jnp.dot(member, per_rollout, precision=lax.Precision.HIGHEST)


def selection(routing, probs, experts, capacity):
    route_hits = (
        routing[:, :, None] == jnp.arange(experts, dtype=jnp.int32)[None, None, :]
    ).astype(jnp.float32)
    occupied = jnp.sum(route_hits, axis=1)
    weight = jnp.einsum("rke,rk->re", route_hits, probs.astype(jnp.float32))
    before = jnp.cumsum(occupied, axis=0) - occupied
    slot_index = jnp.arange(capacity, dtype=jnp.float32)
    chosen = occupied.T[:, None, :] * (before.T[:, None, :] == slot_index[None, :, None]).astype(
        jnp.float32
    )
    return (route_hits, weight, chosen)


def shards(tokens, upstream, probs, routing, row_rollout, group_ids, rewards, w_gate, w_up, w_down):
    experts = lax.axis_size("expert")
    dp_size = lax.axis_size("dp")
    tensor_size = lax.axis_size("tensor")
    group_rows, features = tokens.shape
    routes_per_row = routing.shape[1]
    capacity = min(group_rows, 5 * group_rows * routes_per_row // (4 * experts))
    hidden_width = w_gate.shape[2]
    slots = experts * capacity
    advantage = advantages(row_rollout, group_ids, rewards)
    cotangent = (advantage[:, None] * upstream.astype(jnp.float32)).astype(jnp.bfloat16)
    route_hits, weight, chosen = selection(routing, probs, experts, capacity)
    chosen_half = chosen.astype(jnp.bfloat16)
    packed_rows = jnp.einsum(
        "ecr,rf->ecf", chosen_half, tokens, preferred_element_type=jnp.float32
    ).astype(jnp.bfloat16)
    packed_upstream = jnp.einsum(
        "ecr,rf->ecf", chosen_half, cotangent, preferred_element_type=jnp.float32
    ).astype(jnp.bfloat16)
    packed_prob = jnp.einsum("ecr,re->ec", chosen, weight).astype(jnp.bfloat16)
    arrived = (
        lax.all_to_all(packed_rows, "expert", split_axis=0, concat_axis=0, tiled=True),
        lax.all_to_all(packed_upstream, "expert", split_axis=0, concat_axis=0, tiled=True),
        lax.all_to_all(packed_prob, "expert", split_axis=0, concat_axis=0, tiled=True),
    )
    gathered = (
        lax.all_gather(
            arrived[0].reshape(1, slots, features), ("dp", "tensor"), axis=0, tiled=True
        ),
        lax.all_gather(
            arrived[1].reshape(1, slots, features), ("dp", "tensor"), axis=0, tiled=True
        ),
        lax.all_gather(arrived[2].reshape(1, slots), ("dp", "tensor"), axis=0, tiled=True),
    )
    rows_in = gathered[0].reshape(dp_size, tensor_size, experts, capacity, features)
    rows_back = gathered[1].reshape(dp_size, tensor_size, experts, capacity, features)
    slot_prob = gathered[2].reshape(dp_size, tensor_size, experts, capacity)[:, 0]
    layout = "dtecf"
    weights_in = jnp.concatenate([w_gate[0], w_up[0]], axis=1).reshape(
        tensor_size, features, 2 * hidden_width
    )
    weights_out = w_down[0].reshape(hidden_width, tensor_size, features)
    both = jnp.einsum(
        layout + ",tfk->deck", rows_in, weights_in, preferred_element_type=jnp.float32
    )
    gate = both[..., :hidden_width]
    up_part = both[..., hidden_width:]
    back_hidden = jnp.einsum(
        layout + ",htf->dech", rows_back, weights_out, preferred_element_type=jnp.float32
    )
    sigmoid_gate = jax.nn.sigmoid(gate)
    active = gate * sigmoid_gate
    hidden = (active * up_part).astype(jnp.bfloat16)
    hidden_wide = lax.optimization_barrier(hidden).astype(jnp.float32)
    route_part = jnp.sum(hidden_wide * back_hidden, axis=-1)
    scale = slot_prob.astype(jnp.float32)[..., None]
    scaled = scale * back_hidden
    grad_gate_in = scaled * up_part * sigmoid_gate * (1.0 + gate * (1.0 - sigmoid_gate))
    grad_up_in = scaled * active
    grad_inner = jnp.concatenate([grad_gate_in, grad_up_in], axis=-1).astype(jnp.bfloat16)
    weighted = (scale * hidden_wide).astype(jnp.bfloat16)
    grad_down = jnp.einsum(
        "dech," + layout + "->htf", weighted, rows_back, preferred_element_type=jnp.float32
    )
    grad_down = grad_down.reshape(hidden_width, tensor_size * features).astype(jnp.bfloat16)
    grad_both = jnp.einsum(
        layout + ",deck->tfk", rows_in, grad_inner, preferred_element_type=jnp.float32
    )
    grad_both = grad_both.reshape(tensor_size * features, 2 * hidden_width)
    grad_gate = grad_both[:, :hidden_width].astype(jnp.bfloat16)
    grad_up = grad_both[:, hidden_width:].astype(jnp.bfloat16)
    route_total = lax.psum(route_part, ("dp", "tensor"))
    own_route = lax.dynamic_index_in_dim(route_total, lax.axis_index("dp"), 0, keepdims=False)
    first = jnp.int32(0) // slots
    needed = min(
        dp_size,
        (slots * lax.axis_size(("dp", "tensor")) // slots + tensor_size - 1) // tensor_size + 1,
    )
    lead = jnp.clip(first // tensor_size, 0, dp_size - needed)
    part = lax.dynamic_slice_in_dim(grad_inner, lead, needed, 0)
    product = jnp.einsum("deck,tfk->dtecf", part, weights_in, preferred_element_type=jnp.float32)
    product = product.reshape(needed * tensor_size * slots, features)
    own_rows = lax.psum_scatter(
        product.astype(jnp.bfloat16), ("dp", "tensor"), scatter_dimension=0, tiled=True
    ).astype(jnp.float32)
    home = (
        lax.all_to_all(
            own_rows.reshape(experts, capacity, features).astype(jnp.bfloat16),
            "expert",
            split_axis=0,
            concat_axis=0,
            tiled=True,
        ),
        lax.all_to_all(
            own_route.astype(jnp.bfloat16), "expert", split_axis=0, concat_axis=0, tiled=True
        ),
    )
    input_grad = jnp.einsum(
        "ecr,ecf->rf", chosen_half, home[0], preferred_element_type=jnp.float32
    ).astype(jnp.bfloat16)
    per_expert = jnp.einsum("ecr,ec->re", chosen, home[1].astype(jnp.float32))
    route_grad = jnp.einsum("rke,re->rk", route_hits, per_expert).astype(jnp.bfloat16)
    return (input_grad, route_grad, grad_gate[None], grad_up[None], grad_down[None])


def solution(mesh):
    in_specs = (
        P(("dp", "expert"), "tensor"),
        P(("dp", "expert"), "tensor"),
        P(("dp", "expert"), None),
        P(("dp", "expert"), None),
        P(("dp", "expert")),
        P(),
        P(),
        P("expert", None, ("dp", "tensor")),
        P("expert", None, ("dp", "tensor")),
        P("expert", ("dp", "tensor"), None),
    )
    out_specs = (
        P(("dp", "expert"), "tensor"),
        P(("dp", "expert"), None),
        P("expert", None, ("dp", "tensor")),
        P("expert", None, ("dp", "tensor")),
        P("expert", ("dp", "tensor"), None),
    )
    return jax.shard_map(shards, mesh=mesh, in_specs=in_specs, out_specs=out_specs, check_vma=False)
```

profile of v0, /device:TPU:35, one launch (start us, length us, event | category | flops | bytes accessed | tf_op | source)
XLA Modules:
  0.0 505.4 jit_solution(11312434241959555918)
XLA Ops:
  7.2 0.0 copy-start
  7.2 0.0 copy-start.5
  7.2 0.0 all-gather.6.cloned.1.call-start
  7.3 0.9 convert_reduce_fusion
  8.2 0.3 convolution_convert_fusion
  8.6 0.3 copy.58
  8.9 35.1 %all_to_all.33 = bf16[16,5,3584]{2,1,0:T(8,128)(2,1)S(1)} all-to-all(bf16[16,5,3584]{2,1,0:T(8,128)(2,1)S(1)} %copy.58), channel_id=1, replica_groups=mesh['dp'=8,'expert'=16,'tensor'=2] {'expert'}, dimensions={0} | all-to-all | bytes 1146880 | tf_op jit(solution)/shard_map/all_to_all | solution.py:54
  44.0 1.0 reshape.75
  45.1 0.0 all-gather.6.cloned.1.call-update
  45.1 0.0 all-gather.4.cloned.1.call-start
  45.2 0.7 convert_element_type.94
  45.8 0.9 fusion.41
  46.8 1.0 fusion.34
  47.8 0.8 divide_subtract_fusion
  48.5 0.8 convolution_bitcast_fusion.2
  49.4 1.2 convolution_convert_fusion.1
  50.6 0.3 copy.54
  50.9 30.4 %all_to_all.34 = bf16[16,5,3584]{2,1,0:T(8,128)(2,1)S(1)} all-to-all(bf16[16,5,3584]{2,1,0:T(8,128)(2,1)S(1)} %copy.54), channel_id=1, replica_groups=mesh['dp'=8,'expert'=16,'tensor'=2] {'expert'}, dimensions={0} | all-to-all | bytes 1146880 | tf_op jit(solution)/shard_map/all_to_all | solution.py:55
  81.3 1.0 reshape.73
  82.3 0.0 all-gather.4.cloned.1.call-update
  82.4 0.2 fusion.51
  82.6 0.7 copy.52
  83.3 4.2 all-to-all-start
  87.5 0.0 reduce-scatter.2.cloned.1.call-start
  87.5 2.3 reshape_squeeze.3
  89.8 6.4 %all-to-all-done = bf16[16,1,5]{2,1,0:T(2,128)(2,1)S(1)} async-done(((bf16[16,1,5]{2,1,0:T(2,128)(2,1)}), bf16[16,1,5]{2,1,0:T(2,128)(2,1)S(1)}, u32[]{:S(2)}, u32[]{:S(2)}) %all-to-all-start) | async-done | bytes 192 | tf_op jit(solution)/shard_map/all_to_all | solution.py:56
  96.2 0.1 reshape.78
  96.3 29.7 %all-gather = bf16[16,1,80]{2,1,0:T(2,128)(2,1)S(1)} all-gather(bf16[1,1,80]{2,1,0:T(2,128)(2,1)S(1)} %reshape.78), channel_id=1, replica_groups=mesh['dp'=8,'expert'=16,'tensor'=2] {'dp','tensor'}, dimensions={0}, use_global_device_ids=true | all-gather | bytes 2720 | tf_op jit(solution)/shard_map/all_gather | solution.py:65
  126.1 0.1 reshape.72
  126.3 0.1 copy.53
  126.4 0.0 all-gather.6.cloned.1.call-done
  126.4 12.1 %copy.59 = bf16[16,80,3584]{2,0,1:T(8,128)(2,1)} copy(bf16[16,80,3584]{2,1,0:T(8,128)(2,1)} %all-gather.6.cloned.1.call-done) | data formatting | bytes 18350080 | tf_op jit(solution)/shard_map/all_gather | solution.py:59
  138.5 13.8 %reshape.76 = bf16[8,2,16,5,3584]{4,1,0,3,2:T(2,128)(2,1)} reshape(bf16[16,80,3584]{2,0,1:T(8,128)(2,1)} %copy.59) | data formatting | bytes 18350080 | tf_op jit(solution)/shard_map/reshape | solution.py:67
  152.3 35.1 %all-gather.4.cloned.1.call-done = bf16[16,80,3584]{2,1,0:T(8,128)(2,1)} async-done(((bf16[1,80,3584]{2,1,0:T(8,128)(2,1)}), bf16[16,80,3584]{2,1,0:T(8,128)(2,1)}) %all-gather.4.cloned.1.call-update) | async-done | bytes 9175056 | tf_op jit(solution)/shard_map/all_gather | solution.py:62
  187.4 12.1 %copy.55 = bf16[16,80,3584]{2,0,1:T(8,128)(2,1)} copy(bf16[16,80,3584]{2,1,0:T(8,128)(2,1)} %all-gather.4.cloned.1.call-done) | data formatting | bytes 18350080 | tf_op jit(solution)/shard_map/all_gather | solution.py:62
  199.5 13.9 %reshape.74 = bf16[8,2,16,5,3584]{4,1,0,3,2:T(2,128)(2,1)} reshape(bf16[16,80,3584]{2,0,1:T(8,128)(2,1)} %copy.55) | data formatting | bytes 18350080 | tf_op jit(solution)/shard_map/reshape | solution.py:68
  213.4 0.0 copy-start.4
  213.4 9.5 %fusion.23 = f32[8,16,5,256]{3,1,2,0:T(8,128)S(1)} fusion(bf16[2,3584,128]{2,1,0:T(8,128)(2,1)S(1)} %bitcast.121, bf16[2,3584,128]{2,1,0:T(8,128)(2,1)} %bitcast.123, bf16[8,2,16,5,3584]{4,1,0,3,2:T(2,128)(2,1)} %reshape.76), kind=kOutput, calls=%fused_computation.23 | convolution fusion | flops 2356150272 | bytes 13500416 | tf_op jit(solution)/shard_map/dtecf,tfk->deck/dot_general | solution.py:75
  222.9 0.0 copy-start.7
  222.9 5.1 %multiply_convert_fusion.2 = (bf16[8,16,5,128]{3,1,2,0:T(8,128)(2,1)S(1)}, bf16[8,16,5,128]{3,1,2,0:T(8,128)(2,1)S(1)}, bf16[8,16,5,128]{3,1,2,0:T(8,128)(2,1)S(1)}, f32[8,16,5,128]{3,1,2,0:T(8,128)S(1)}) fusion(f32[8,16,5,256]{3,1,2,0:T(8,128)S(1)} %fusion.23, f32[8,16,5]{1,2,0:T(8,128)S(1)} %copy.53, bf16[128,2,3584,1,1]{2,1,0,4,3:T(2,128)(2,1)S(1)} %bitcast.108, ...), kind=kOutput, calls=%fused_computation.39 | convolution fusion | flops 1175715840 | bytes 12487168 | tf_op jit(solution)/shard_map/dtecf,htf->dech/dot_general | solution.py:80
  228.0 3.0 convert_bitcast_fusion
  231.1 11.2 %copy.61 = bf16[8,2,16,5,3584]{4,3,2,1,0:T(8,128)(2,1)} copy(bf16[8,2,16,5,3584]{4,2,3,0,1:T(8,128)(2,1)S(1)} %convert_bitcast_fusion) | data formatting | bytes 18350080 | tf_op jit(solution)/shard_map/convert_element_type | solution.py:116
  242.3 14.9 %convert_element_type.102 = bf16[1280,3584]{1,0:T(8,128)(2,1)} reshape(bf16[8,2,16,5,3584]{4,3,2,1,0:T(8,128)(2,1)} %copy.61) | data formatting | bytes 18350080 | tf_op jit(solution)/shard_map/convert_element_type | solution.py:116
  257.2 0.0 reduce-scatter.2.cloned.1.call-update
  257.2 15.2 %reshape.104 = bf16[7168,5,8,16]{0,2,1,3:T(8,128)(2,1)} reshape(bf16[2,3584,5,8,16]{1,0,3,2,4:T(2,128)(2,1)} %bitcast.107) | data formatting | bytes 18350080 | tf_op jit(solution)/shard_map/dtecf,deck->tfk/dot_general | solution.py:98
  272.4 0.3 fusion.37
  272.7 51.8 %psum.7 = bf16[8,16,5]{1,2,0:T(8,128)(2,1)S(1)} all-reduce(f32[8,16,5]{1,2,0:T(8,128)S(1)} %get-tuple-element.11), channel_id=1, replica_groups=mesh['dp'=8,'expert'=16,'tensor'=2] {'dp','tensor'}, use_global_device_ids=true, to_apply=%region_5.6 | all-reduce | flops 640 | bytes 3840 | tf_op jit(solution)/shard_map/psum | solution.py:104
  324.5 0.7 copy.63
  325.2 8.6 %all-to-all-start.4 = ((bf16[16,1,5]{2,1,0:T(2,128)(2,1)}), bf16[16,1,5]{2,1,0:T(2,128)(2,1)S(1)}, u32[]{:S(2)}, u32[]{:S(2)}) async-start(bf16[16,1,5]{2,1,0:T(2,128)(2,1)} %copy.63), calls=%async_computation.5 | async-start | bytes 16384 | tf_op jit(solution)/shard_map/all_to_all | solution.py:126
  333.8 10.7 %fusion.7 = bf16[7168,256]{1,0:T(8,128)(2,1)S(1)} fusion(bf16[7168,5,8,16]{0,2,1,3:T(8,128)(2,1)} %reshape.104, bf16[8,16,5,128]{3,1,2,0:T(8,128)(2,1)S(1)} %get-tuple-element.8, bf16[8,16,5,128]{3,1,2,0:T(8,128)(2,1)S(1)} %get-tuple-element.7), kind=kOutput, calls=%fused_computation.9 | convolution fusion | flops 2351300608 | bytes 13172736 | tf_op jit(solution)/shard_map/dtecf,deck->tfk/dot_general | solution.py:98
  344.5 2.1 slice_bitcast_fusion
  346.6 15.2 %reshape.105 = bf16[7168,5,8,16]{0,2,1,3:T(8,128)(2,1)} reshape(bf16[2,3584,5,8,16]{1,0,3,2,4:T(2,128)(2,1)} %bitcast.106) | data formatting | bytes 18350080 | tf_op jit(solution)/shard_map/dech,dtecf->htf/dot_general | solution.py:94
  361.8 97.4 %reduce-scatter.2.cloned.1.call-done = bf16[80,3584]{1,0:T(8,128)(2,1)} async-done(((bf16[1280,3584]{1,0:T(8,128)(2,1)}), bf16[80,3584]{1,0:T(8,128)(2,1)}) %reduce-scatter.2.cloned.1.call-update) | async-done | bytes 573456 | tf_op jit(solution)/shard_map/reduce_scatter | solution.py:115
  459.2 2.2 convert_element_type.103
  461.4 0.0 all-to-all-done.4
  461.4 9.5 %all-to-all-start.3 = ((bf16[16,5,3584]{2,1,0:T(8,128)(2,1)}), bf16[16,5,3584]{2,1,0:T(8,128)(2,1)S(1)}, u32[]{:S(2)}, u32[]{:S(2)}) async-start(bf16[16,5,3584]{2,1,0:T(8,128)(2,1)} %convert_element_type.103), calls=%async_computation.4 | async-start | bytes 1835008 | tf_op jit(solution)/shard_map/all_to_all | solution.py:119
  471.0 10.6 %fusion.16 = bf16[1,128,7168]{2,1,0:T(8,128)(2,1)} fusion(bf16[7168,5,8,16]{0,2,1,3:T(8,128)(2,1)} %reshape.105, bf16[8,16,5,128]{3,1,2,0:T(8,128)(2,1)S(1)} %get-tuple-element.10), kind=kOutput, calls=%fused_computation.12 | convolution fusion | flops 1175322624 | bytes 11173888 | tf_op jit(solution)/shard_map/dech,dtecf->htf/dot_general | solution.py:94
  481.6 0.1 copy.98
  481.7 0.1 copy.86
  481.8 0.1 copy.87
  481.9 0.2 fusion.50
  482.1 0.6 convert_element_type.109
  482.7 15.0 %all-to-all-done.3 = bf16[16,5,3584]{2,1,0:T(8,128)(2,1)S(1)} async-done(((bf16[16,5,3584]{2,1,0:T(8,128)(2,1)}), bf16[16,5,3584]{2,1,0:T(8,128)(2,1)S(1)}, u32[]{:S(2)}, u32[]{:S(2)}) %all-to-all-start.3) | async-done | bytes 573472 | tf_op jit(solution)/shard_map/all_to_all | solution.py:119
  497.7 0.9 fusion.19
  (23 shorter events, 0.2 us)
Async XLA Ops:
  7.2 1.0 copy-start
  7.2 75.2 %copy-start.5 = (s32[8,8]{1,0:T(8,128)S(1)}, s32[8,8]{1,0:T(8,128)}, u32[]{:S(2)}) copy-start(s32[8,8]{1,0:T(8,128)} %param.13) | copy-start | bytes 772
  7.2 75.2 %copy-start.8 = (bf16[8,8]{1,0:T(8,128)(2,1)S(1)}, bf16[8,8]{1,0:T(8,128)(2,1)}, u32[]{:S(2)}) copy-start(bf16[8,8]{1,0:T(8,128)(2,1)} %param.12) | copy-start | bytes 388
  7.2 80.3 %copy-start.3 = (bf16[1,128,7168]{2,1,0:T(8,128)(2,1)S(1)}, bf16[1,128,7168]{2,1,0:T(8,128)(2,1)}, u32[]{:S(2)}) copy-start(bf16[1,128,7168]{2,1,0:T(8,128)(2,1)} %param.19) | copy-start | bytes 5505028
  7.2 119.2 %all-gather.6.cloned.1.call-start = ((), (), s32[]{:S(2)}) async-start(), calls=%async_computation.7 | async-start | bytes 9748480 | tf_op jit(solution)/shard_map/all_gather | solution.py:59
  45.1 142.3 %all-gather.4.cloned.1.call-start = ((), (), s32[]{:S(2)}) async-start(), calls=%async_computation.6 | async-start | bytes 9748480 | tf_op jit(solution)/shard_map/all_gather | solution.py:62
  83.3 12.9 %all-to-all-start = ((bf16[16,1,5]{2,1,0:T(2,128)(2,1)}), bf16[16,1,5]{2,1,0:T(2,128)(2,1)S(1)}, u32[]{:S(2)}, u32[]{:S(2)}) async-start(bf16[16,1,5]{2,1,0:T(2,128)(2,1)} %copy.52), calls=%async_computation | async-start | bytes 16384 | tf_op jit(solution)/shard_map/all_to_all | solution.py:56
  87.5 371.7 %reduce-scatter.2.cloned.1.call-start = ((), (), s32[]{:S(2)}) async-start(), calls=%async_computation.8 | async-start | bytes 9748480 | tf_op jit(solution)/shard_map/reduce_scatter | solution.py:115
  199.5 13.9 %copy-start.6 = (bf16[1,7168,128]{2,1,0:T(8,128)(2,1)S(1)}, bf16[1,7168,128]{2,1,0:T(8,128)(2,1)}, u32[]{:S(2)}) copy-start(bf16[1,7168,128]{2,1,0:T(8,128)(2,1)} %param.18) | copy-start | bytes 5505028
  213.4 9.6 %copy-start.2 = (bf16[8,2,16,5,3584]{4,1,0,3,2:T(2,128)(2,1)S(1)}, bf16[8,2,16,5,3584]{4,1,0,3,2:T(2,128)(2,1)}, u32[]{:S(2)}) copy-start(bf16[8,2,16,5,3584]{4,1,0,3,2:T(2,128)(2,1)} %reshape.74) | copy-start | bytes 27525124
  213.4 9.6 %copy-start.4 = (bf16[128,2,3584]{2,1,0:T(2,128)(2,1)S(1)}, bf16[128,2,3584]{2,1,0:T(2,128)(2,1)}, u32[]{:S(2)}) copy-start(bf16[128,2,3584]{2,1,0:T(2,128)(2,1)} %reshape_squeeze.3) | copy-start | bytes 5505028
  222.9 5.1 %copy-start.7 = (bf16[1,7168,128]{2,1,0:T(8,128)(2,1)S(1)}, bf16[1,7168,128]{2,1,0:T(8,128)(2,1)}, u32[]{:S(2)}) copy-start(bf16[1,7168,128]{2,1,0:T(8,128)(2,1)} %param.17) | copy-start | bytes 5505028
  325.2 136.2 %all-to-all-start.4 = ((bf16[16,1,5]{2,1,0:T(2,128)(2,1)}), bf16[16,1,5]{2,1,0:T(2,128)(2,1)S(1)}, u32[]{:S(2)}, u32[]{:S(2)}) async-start(bf16[16,1,5]{2,1,0:T(2,128)(2,1)} %copy.63), calls=%async_computation.5 | async-start | bytes 16384 | tf_op jit(solution)/shard_map/all_to_all | solution.py:126
  346.6 152.1 %copy-start.1 = (bf16[8,3584]{1,0:T(8,128)(2,1)S(1)}, bf16[8,3584]{1,0:T(8,128)(2,1)}, u32[]{:S(2)}) copy-start(bf16[8,3584]{1,0:T(8,128)(2,1)} %param.10) | copy-start | bytes 172036
  461.4 36.3 %all-to-all-start.3 = ((bf16[16,5,3584]{2,1,0:T(8,128)(2,1)}), bf16[16,5,3584]{2,1,0:T(8,128)(2,1)S(1)}, u32[]{:S(2)}, u32[]{:S(2)}) async-start(bf16[16,5,3584]{2,1,0:T(8,128)(2,1)} %convert_element_type.103), calls=%async_computation.4 | async-start | bytes 1835008 | tf_op jit(solution)/shard_map/all_to_all | solution.py:119
Sparse Core Ops, SparseCore 0:
  45.2 76.4 all-gather.5
  124.1 63.2 all-gather.3
  257.3 201.8 reduce-scatter.1
where the time goes:
time: 511 us; the launch traced here: 505 us
  waiting for transfers between devices  154 us (30%)
  blocking collectives  147 us (29%)
  local copies, waits for them, and re-layouts  120 us (23%)
  matrix products  43.7 us (9%)
  starting transfers between devices  22.4 us (4%)
  between operations  14.3 us (3%)
    reduce_scatter x1, waiting for transfers between devices, shards(): lax.psum_scatter(product.astype(jnp.bfloat16), ('dp', 'tensor'), scatter_...  97.4 us
    psum x1, blocking collectives, shards(): route_total = lax.psum(route_part, ('dp', 'tensor'))  51.8 us
    all_to_all x1, blocking collectives, shards(): lax.all_to_all(packed_rows, 'expert', split_axis=0, concat_axis=0, tiled=...  35.1 us
    all_gather x1, waiting for transfers between devices, shards(): lax.all_gather(arrived[1].reshape(1, slots, features), ('dp', 'tensor'),...  35.1 us
    all_to_all x1, blocking collectives, shards(): lax.all_to_all(packed_upstream, 'expert', split_axis=0, concat_axis=0, ti...  30.4 us
    all_gather x1, blocking collectives, shards(): lax.all_gather(arrived[2].reshape(1, slots), ('dp', 'tensor'), axis=0, ti...  29.7 us
    convert_element_type x2, local copies, waits for them, and re-layouts, shards(): product.astype(jnp.bfloat16)  26.1 us
    dot_general x1, local copies, waits for them, and re-layouts, shards(): jnp.einsum('dech,' + layout + '->htf', weighted, rows_back, preferred_ele...  15.2 us
  transfers between devices with their start and end apart: 6, of which 4 were waited for; matrix products, arithmetic and copies ran while one was open for 19% of the time, Pallas kernels for 0%

commit v1 on v0

--- a/solution.py
+++ b/solution.py
@@ -101,7 +101,7 @@
     grad_both = grad_both.reshape(tensor_size * features, 2 * hidden_width)
     grad_gate = grad_both[:, :hidden_width].astype(jnp.bfloat16)
     grad_up = grad_both[:, hidden_width:].astype(jnp.bfloat16)
-    route_total = lax.psum(route_part, ("dp", "tensor"))
+    route_total = jnp.sum(lax.all_gather(route_part, ("dp", "tensor")), axis=0)
     own_route = lax.dynamic_index_in_dim(route_total, lax.axis_index("dp"), 0, keepdims=False)
     first = jnp.int32(0) // slots
     needed = min(

time: 511 us -> 513 us (level)
  waiting for transfers between devices: 154 us -> 178 us
  blocking collectives: 147 us -> 124 us
    psum x1 -> x0, blocking collectives: 51.8 us -> none  [shards(): route_total = lax.psum(route_part, ('dp', 'tensor'))]
    all_gather x0 -> x1, blocking collectives: none -> 28.4 us  [shards(): route_total = jnp.sum(lax.all_gather(route_part, ('dp', 'tensor')), axis=0)]
    reduce_scatter x1, waiting for transfers between devices: 97.4 us -> 121 us  [shards(): lax.psum_scatter(product.astype(jnp.bfloat16), ('dp', 'tensor'), scatter_...]
where the time goes in v1:
time: 513 us; the launch traced here: 506 us
  waiting for transfers between devices  178 us (35%)
  blocking collectives  124 us (24%)
  local copies, waits for them, and re-layouts  120 us (23%)
  matrix products  43.7 us (9%)
  starting transfers between devices  22.5 us (4%)
  between operations  14.3 us (3%)
    reduce_scatter x1, waiting for transfers between devices, shards(): lax.psum_scatter(product.astype(jnp.bfloat16), ('dp', 'tensor'), scatter_...  121 us
    all_to_all x1, blocking collectives, shards(): lax.all_to_all(packed_rows, 'expert', split_axis=0, concat_axis=0, tiled=...  35.1 us
    all_gather x1, waiting for transfers between devices, shards(): lax.all_gather(arrived[1].reshape(1, slots, features), ('dp', 'tensor'),...  35.1 us
    all_to_all x1, blocking collectives, shards(): lax.all_to_all(packed_upstream, 'expert', split_axis=0, concat_axis=0, ti...  30.4 us
    all_gather x1, blocking collectives, shards(): lax.all_gather(arrived[2].reshape(1, slots), ('dp', 'tensor'), axis=0, ti...  29.7 us
    all_gather x1, blocking collectives, shards(): route_total = jnp.sum(lax.all_gather(route_part, ('dp', 'tensor')), axis=0)  28.4 us
    convert_element_type x2, local copies, waits for them, and re-layouts, shards(): product.astype(jnp.bfloat16)  26.1 us
    dot_general x1, local copies, waits for them, and re-layouts, shards(): jnp.einsum(layout + ',deck->tfk', rows_in, grad_inner, preferred_element_...  15.2 us
  transfers between devices with their start and end apart: 6, of which 4 were waited for; matrix products, arithmetic and copies ran while one was open for 19% of the time, Pallas kernels for 0%

profile of v1, /device:TPU:35, one launch (start us, length us, event | category | flops | bytes accessed | tf_op | source)
XLA Modules:
  0.0 505.8 jit_solution(16180355695597725093)
XLA Ops:
  7.2 0.0 copy-start
  7.2 0.0 copy-start.5
  7.2 0.0 all-gather.7.cloned.1.call-start
  7.3 0.9 convert_reduce_fusion
  8.2 0.3 convolution_convert_fusion
  8.6 0.3 copy.95
  8.9 35.1 %all_to_all.33 = bf16[16,5,3584]{2,1,0:T(8,128)(2,1)S(1)} all-to-all(bf16[16,5,3584]{2,1,0:T(8,128)(2,1)S(1)} %copy.95), channel_id=1, replica_groups=mesh['dp'=8,'expert'=16,'tensor'=2] {'expert'}, dimensions={0} | all-to-all | bytes 1146880 | tf_op jit(solution)/shard_map/all_to_all | solution.py:54
  44.0 1.0 reshape.75
  45.1 0.0 all-gather.7.cloned.1.call-update
  45.1 0.0 all-gather.5.cloned.1.call-start
  45.2 0.7 convert_element_type.94
  45.8 0.9 fusion.41
  46.8 1.0 fusion.34
  47.8 0.8 divide_subtract_fusion
  48.5 0.8 convolution_bitcast_fusion.2
  49.4 1.2 convolution_convert_fusion.1
  50.6 0.3 copy.91
  50.9 30.4 %all_to_all.34 = bf16[16,5,3584]{2,1,0:T(8,128)(2,1)S(1)} all-to-all(bf16[16,5,3584]{2,1,0:T(8,128)(2,1)S(1)} %copy.91), channel_id=1, replica_groups=mesh['dp'=8,'expert'=16,'tensor'=2] {'expert'}, dimensions={0} | all-to-all | bytes 1146880 | tf_op jit(solution)/shard_map/all_to_all | solution.py:55
  81.3 1.0 reshape.73
  82.3 0.0 all-gather.5.cloned.1.call-update
  82.4 0.2 fusion.51
  82.6 0.7 copy.89
  83.3 4.2 all-to-all-start
  87.5 0.0 reduce-scatter.2.cloned.1.call-start
  87.5 2.3 reshape_squeeze.3
  89.8 6.4 %all-to-all-done = bf16[16,1,5]{2,1,0:T(2,128)(2,1)S(1)} async-done(((bf16[16,1,5]{2,1,0:T(2,128)(2,1)}), bf16[16,1,5]{2,1,0:T(2,128)(2,1)S(1)}, u32[]{:S(2)}, u32[]{:S(2)}) %all-to-all-start) | async-done | bytes 192 | tf_op jit(solution)/shard_map/all_to_all | solution.py:56
  96.2 0.1 reshape.79
  96.3 29.7 %all-gather.1 = bf16[16,1,80]{2,1,0:T(2,128)(2,1)S(1)} all-gather(bf16[1,1,80]{2,1,0:T(2,128)(2,1)S(1)} %reshape.79), channel_id=1, replica_groups=mesh['dp'=8,'expert'=16,'tensor'=2] {'dp','tensor'}, dimensions={0}, use_global_device_ids=true | all-gather | bytes 2720 | tf_op jit(solution)/shard_map/all_gather | solution.py:65
  126.1 0.1 reshape.72
  126.3 0.1 copy.90
  126.4 0.0 all-gather.7.cloned.1.call-done
  126.4 12.1 %copy.96 = bf16[16,80,3584]{2,0,1:T(8,128)(2,1)} copy(bf16[16,80,3584]{2,1,0:T(8,128)(2,1)} %all-gather.7.cloned.1.call-done) | data formatting | bytes 18350080 | tf_op jit(solution)/shard_map/all_gather | solution.py:59
  138.5 13.8 %reshape.76 = bf16[8,2,16,5,3584]{4,1,0,3,2:T(2,128)(2,1)} reshape(bf16[16,80,3584]{2,0,1:T(8,128)(2,1)} %copy.96) | data formatting | bytes 18350080 | tf_op jit(solution)/shard_map/reshape | solution.py:67
  152.3 35.1 %all-gather.5.cloned.1.call-done = bf16[16,80,3584]{2,1,0:T(8,128)(2,1)} async-done(((bf16[1,80,3584]{2,1,0:T(8,128)(2,1)}), bf16[16,80,3584]{2,1,0:T(8,128)(2,1)}) %all-gather.5.cloned.1.call-update) | async-done | bytes 9175056 | tf_op jit(solution)/shard_map/all_gather | solution.py:62
  187.4 12.1 %copy.92 = bf16[16,80,3584]{2,0,1:T(8,128)(2,1)} copy(bf16[16,80,3584]{2,1,0:T(8,128)(2,1)} %all-gather.5.cloned.1.call-done) | data formatting | bytes 18350080 | tf_op jit(solution)/shard_map/all_gather | solution.py:62
  199.5 13.9 %reshape.74 = bf16[8,2,16,5,3584]{4,1,0,3,2:T(2,128)(2,1)} reshape(bf16[16,80,3584]{2,0,1:T(8,128)(2,1)} %copy.92) | data formatting | bytes 18350080 | tf_op jit(solution)/shard_map/reshape | solution.py:68
  213.4 0.0 copy-start.4
  213.4 9.5 %fusion.23 = f32[8,16,5,256]{3,1,2,0:T(8,128)S(1)} fusion(bf16[2,3584,128]{2,1,0:T(8,128)(2,1)S(1)} %bitcast.125, bf16[2,3584,128]{2,1,0:T(8,128)(2,1)} %bitcast.127, bf16[8,2,16,5,3584]{4,1,0,3,2:T(2,128)(2,1)} %reshape.76), kind=kOutput, calls=%fused_computation.23 | convolution fusion | flops 2356150272 | bytes 13500416 | tf_op jit(solution)/shard_map/dtecf,tfk->deck/dot_general | solution.py:75
  222.9 0.0 copy-start.7
  222.9 5.1 %multiply_convert_fusion.2 = (bf16[8,16,5,128]{3,1,2,0:T(8,128)(2,1)S(1)}, bf16[8,16,5,128]{3,1,2,0:T(8,128)(2,1)S(1)}, bf16[8,16,5,128]{3,1,2,0:T(8,128)(2,1)S(1)}, f32[8,16,5,128]{3,1,2,0:T(8,128)S(1)}) fusion(f32[8,16,5,256]{3,1,2,0:T(8,128)S(1)} %fusion.23, f32[8,16,5]{1,2,0:T(8,128)S(1)} %copy.90, bf16[128,2,3584,1,1]{2,1,0,4,3:T(2,128)(2,1)S(1)} %bitcast.111, ...), kind=kOutput, calls=%fused_computation.40 | convolution fusion | flops 1175715840 | bytes 12487168 | tf_op jit(solution)/shard_map/dtecf,htf->dech/dot_general | solution.py:80
  228.0 3.0 convert_bitcast_fusion
  231.1 11.2 %copy.98 = bf16[8,2,16,5,3584]{4,3,2,1,0:T(8,128)(2,1)} copy(bf16[8,2,16,5,3584]{4,2,3,0,1:T(8,128)(2,1)S(1)} %convert_bitcast_fusion) | data formatting | bytes 18350080 | tf_op jit(solution)/shard_map/convert_element_type | solution.py:116
  242.3 14.9 %convert_element_type.102 = bf16[1280,3584]{1,0:T(8,128)(2,1)} reshape(bf16[8,2,16,5,3584]{4,3,2,1,0:T(8,128)(2,1)} %copy.98) | data formatting | bytes 18350080 | tf_op jit(solution)/shard_map/convert_element_type | solution.py:116
  257.2 0.0 reduce-scatter.2.cloned.1.call-update
  257.2 0.3 fusion.37
  257.5 28.4 %all-gather = f32[128,16,5]{1,0,2:T(8,128)S(1)} all-gather(f32[8,16,5]{1,0,2:T(8,128)S(1)} %copy.100), channel_id=2, replica_groups=mesh['dp'=8,'expert'=16,'tensor'=2] {'dp','tensor'}, dimensions={0}, use_global_device_ids=true | all-gather | bytes 43520 | tf_op jit(solution)/shard_map/all_gather | solution.py:104
  286.0 0.7 copy.101
  286.7 8.9 %all-to-all-start.4 = ((bf16[16,1,5]{2,1,0:T(2,128)(2,1)}), bf16[16,1,5]{2,1,0:T(2,128)(2,1)S(1)}, u32[]{:S(2)}, u32[]{:S(2)}) async-start(bf16[16,1,5]{2,1,0:T(2,128)(2,1)} %copy.101), calls=%async_computation.5 | async-start | bytes 16384 | tf_op jit(solution)/shard_map/all_to_all | solution.py:126
  295.6 15.2 %reshape.105 = bf16[7168,5,8,16]{0,2,1,3:T(8,128)(2,1)} reshape(bf16[2,3584,5,8,16]{1,0,3,2,4:T(2,128)(2,1)} %bitcast.110) | data formatting | bytes 18350080 | tf_op jit(solution)/shard_map/dtecf,deck->tfk/dot_general | solution.py:98
  310.8 10.7 %fusion.7 = bf16[7168,256]{1,0:T(8,128)(2,1)S(1)} fusion(bf16[7168,5,8,16]{0,2,1,3:T(8,128)(2,1)} %reshape.105, bf16[8,16,5,128]{3,1,2,0:T(8,128)(2,1)S(1)} %get-tuple-element.8, bf16[8,16,5,128]{3,1,2,0:T(8,128)(2,1)S(1)} %get-tuple-element.7), kind=kOutput, calls=%fused_computation.9 | convolution fusion | flops 2351300608 | bytes 13172736 | tf_op jit(solution)/shard_map/dtecf,deck->tfk/dot_general | solution.py:98
  321.5 2.1 slice_bitcast_fusion
  323.6 15.2 %reshape.106 = bf16[7168,5,8,16]{0,2,1,3:T(8,128)(2,1)} reshape(bf16[2,3584,5,8,16]{1,0,3,2,4:T(2,128)(2,1)} %bitcast.109) | data formatting | bytes 18350080 | tf_op jit(solution)/shard_map/dech,dtecf->htf/dot_general | solution.py:94
  338.8 121.2 %reduce-scatter.2.cloned.1.call-done = bf16[80,3584]{1,0:T(8,128)(2,1)} async-done(((bf16[1280,3584]{1,0:T(8,128)(2,1)}), bf16[80,3584]{1,0:T(8,128)(2,1)}) %reduce-scatter.2.cloned.1.call-update) | async-done | bytes 573456 | tf_op jit(solution)/shard_map/reduce_scatter | solution.py:115
  460.0 2.2 convert_element_type.103
  462.2 0.0 all-to-all-done.4
  462.2 9.4 %all-to-all-start.3 = ((bf16[16,5,3584]{2,1,0:T(8,128)(2,1)}), bf16[16,5,3584]{2,1,0:T(8,128)(2,1)S(1)}, u32[]{:S(2)}, u32[]{:S(2)}) async-start(bf16[16,5,3584]{2,1,0:T(8,128)(2,1)} %convert_element_type.103), calls=%async_computation.4 | async-start | bytes 1835008 | tf_op jit(solution)/shard_map/all_to_all | solution.py:119
  471.6 10.6 %fusion.16 = bf16[1,128,7168]{2,1,0:T(8,128)(2,1)} fusion(bf16[7168,5,8,16]{0,2,1,3:T(8,128)(2,1)} %reshape.106, bf16[8,16,5,128]{3,1,2,0:T(8,128)(2,1)S(1)} %get-tuple-element.10), kind=kOutput, calls=%fused_computation.12 | convolution fusion | flops 1175322624 | bytes 11173888 | tf_op jit(solution)/shard_map/dech,dtecf->htf/dot_general | solution.py:94
  482.2 0.1 copy.137
  482.3 0.1 copy.124
  482.4 0.1 copy.125
  482.5 0.2 fusion.50
  482.7 0.6 convert_element_type.109
  483.3 14.8 %all-to-all-done.3 = bf16[16,5,3584]{2,1,0:T(8,128)(2,1)S(1)} async-done(((bf16[16,5,3584]{2,1,0:T(8,128)(2,1)}), bf16[16,5,3584]{2,1,0:T(8,128)(2,1)S(1)}, u32[]{:S(2)}, u32[]{:S(2)}) %all-to-all-start.3) | async-done | bytes 573472 | tf_op jit(solution)/shard_map/all_to_all | solution.py:119
  498.1 0.9 fusion.19
  (26 shorter events, 0.2 us)
Async XLA Ops:
  7.2 1.0 copy-start
  7.2 75.2 %copy-start.5 = (s32[8,8]{1,0:T(8,128)S(1)}, s32[8,8]{1,0:T(8,128)}, u32[]{:S(2)}) copy-start(s32[8,8]{1,0:T(8,128)} %param.13) | copy-start | bytes 772
  7.2 75.2 %copy-start.8 = (bf16[8,8]{1,0:T(8,128)(2,1)S(1)}, bf16[8,8]{1,0:T(8,128)(2,1)}, u32[]{:S(2)}) copy-start(bf16[8,8]{1,0:T(8,128)(2,1)} %param.12) | copy-start | bytes 388
  7.2 80.3 %copy-start.3 = (bf16[1,128,7168]{2,1,0:T(8,128)(2,1)S(1)}, bf16[1,128,7168]{2,1,0:T(8,128)(2,1)}, u32[]{:S(2)}) copy-start(bf16[1,128,7168]{2,1,0:T(8,128)(2,1)} %param.19) | copy-start | bytes 5505028
  7.2 119.2 %all-gather.7.cloned.1.call-start = ((), (), s32[]{:S(2)}) async-start(), calls=%async_computation.7 | async-start | bytes 9748480 | tf_op jit(solution)/shard_map/all_gather | solution.py:59
  45.1 142.3 %all-gather.5.cloned.1.call-start = ((), (), s32[]{:S(2)}) async-start(), calls=%async_computation.6 | async-start | bytes 9748480 | tf_op jit(solution)/shard_map/all_gather | solution.py:62
  83.3 12.9 %all-to-all-start = ((bf16[16,1,5]{2,1,0:T(2,128)(2,1)}), bf16[16,1,5]{2,1,0:T(2,128)(2,1)S(1)}, u32[]{:S(2)}, u32[]{:S(2)}) async-start(bf16[16,1,5]{2,1,0:T(2,128)(2,1)} %copy.89), calls=%async_computation | async-start | bytes 16384 | tf_op jit(solution)/shard_map/all_to_all | solution.py:56
  87.5 372.5 %reduce-scatter.2.cloned.1.call-start = ((), (), s32[]{:S(2)}) async-start(), calls=%async_computation.8 | async-start | bytes 9748480 | tf_op jit(solution)/shard_map/reduce_scatter | solution.py:115
  199.5 13.9 %copy-start.6 = (bf16[1,7168,128]{2,1,0:T(8,128)(2,1)S(1)}, bf16[1,7168,128]{2,1,0:T(8,128)(2,1)}, u32[]{:S(2)}) copy-start(bf16[1,7168,128]{2,1,0:T(8,128)(2,1)} %param.18) | copy-start | bytes 5505028
  213.4 9.6 %copy-start.2 = (bf16[8,2,16,5,3584]{4,1,0,3,2:T(2,128)(2,1)S(1)}, bf16[8,2,16,5,3584]{4,1,0,3,2:T(2,128)(2,1)}, u32[]{:S(2)}) copy-start(bf16[8,2,16,5,3584]{4,1,0,3,2:T(2,128)(2,1)} %reshape.74) | copy-start | bytes 27525124
  213.4 9.6 %copy-start.4 = (bf16[128,2,3584]{2,1,0:T(2,128)(2,1)S(1)}, bf16[128,2,3584]{2,1,0:T(2,128)(2,1)}, u32[]{:S(2)}) copy-start(bf16[128,2,3584]{2,1,0:T(2,128)(2,1)} %reshape_squeeze.3) | copy-start | bytes 5505028
  222.9 5.1 %copy-start.7 = (bf16[1,7168,128]{2,1,0:T(8,128)(2,1)S(1)}, bf16[1,7168,128]{2,1,0:T(8,128)(2,1)}, u32[]{:S(2)}) copy-start(bf16[1,7168,128]{2,1,0:T(8,128)(2,1)} %param.17) | copy-start | bytes 5505028
  286.7 175.4 %all-to-all-start.4 = ((bf16[16,1,5]{2,1,0:T(2,128)(2,1)}), bf16[16,1,5]{2,1,0:T(2,128)(2,1)S(1)}, u32[]{:S(2)}, u32[]{:S(2)}) async-start(bf16[16,1,5]{2,1,0:T(2,128)(2,1)} %copy.101), calls=%async_computation.5 | async-start | bytes 16384 | tf_op jit(solution)/shard_map/all_to_all | solution.py:126
  323.6 175.4 %copy-start.1 = (bf16[8,3584]{1,0:T(8,128)(2,1)S(1)}, bf16[8,3584]{1,0:T(8,128)(2,1)}, u32[]{:S(2)}) copy-start(bf16[8,3584]{1,0:T(8,128)(2,1)} %param.10) | copy-start | bytes 172036
  462.2 35.9 %all-to-all-start.3 = ((bf16[16,5,3584]{2,1,0:T(8,128)(2,1)}), bf16[16,5,3584]{2,1,0:T(8,128)(2,1)S(1)}, u32[]{:S(2)}, u32[]{:S(2)}) async-start(bf16[16,5,3584]{2,1,0:T(8,128)(2,1)} %convert_element_type.103), calls=%async_computation.4 | async-start | bytes 1835008 | tf_op jit(solution)/shard_map/all_to_all | solution.py:119
Sparse Core Ops, SparseCore 0:
  45.2 76.4 all-gather.6
  124.1 63.2 all-gather.4
  257.3 202.5 reduce-scatter.1
